TPU v7x, 128 devices: a whole 4x4x4 slice. The times are simulated.
128 devices in a mesh: gx: 8 (over z, core), gy: 16 (over y, x).
Axes of the slice: x: 4, y: 4, z: 4, core: 2. Of those that a mesh axis runs over, the one named last changes fastest.
Arguments:
- hidden_in: bfloat16 [32768, 3584], P(('gx', 'gy')), may hold values from -6 to 6
- lengths: int32 [8, 4], P('gx'), may hold values from 1 to 2048, 4096 in all within a row
- attn_norm: float32 [3584], replicated, may hold values from 0.5 to 1.5
- qkv_weight: bfloat16 [3584, 4608], P('gx', 'gy'), may hold values from -0.09375 to 0.09375
- qkv_bias: float32 [4608], replicated, may hold values from -5 to 5
Outputs:
- attn: bfloat16 [32768, 3584], P(('gx', 'gy'))
- kv_rows: bfloat16 [32768, 1024], P(('gx', 'gy'))
Inputs may be any that keep to these rules, and one draw needn't show every extreme that they name: Each row of lengths sums to 4096; the longest of each row is exactly 2048.
All inputs are finite; a program needn't handle non-finite values.
Results may differ from a plain program's by a relative error of at most 0.0035.
The roundings to bfloat16 on the way count: a program that leaves them out, or rounds other values in their place, can miss the bound.
Values may be sent and summed in bfloat16 or wider, within the bound.
No kernel may reach another device: no remote copies, remote signals or barrier semaphores. Data moves between devices by JAX's collectives and lax.ppermute only.
A program may use at most 128 MiB of HBM per device.

v0:
```python
import math
import jax
import jax.numpy as jnp
from jax import lax
from jax.sharding import PartitionSpec as P

HEADS = 28
KV_HEADS = 4
HEAD_DIM = 128
key_span = 512


def norm_rows(values, gain):
    wide = values.astype(jnp.float32)
    scale = lax.rsqrt(jnp.mean(wide * wide, axis=1, keepdims=True) + 1e-06)
    return (wide * scale * gain[None, :]).astype(jnp.bfloat16)


def segment_of(index, ends):
    return jnp.sum((ends[None, :] <= index[:, None]).astype(jnp.int32), axis=1)


def rotate(block, pos, heads):
    half = HEAD_DIM // 2
    freqs = 1000000.0 ** (-2.0 * jnp.arange(half, dtype=jnp.float32) / HEAD_DIM)
    angle = pos.astype(jnp.float32)[:, None, None] * freqs[None, None, :]
    wide = block.astype(jnp.float32).reshape(block.shape[0], heads, HEAD_DIM)
    first, second = (wide[..., :half], wide[..., half:])
    turned = jnp.concatenate(
        [
            first * jnp.cos(angle) - second * jnp.sin(angle),
            second * jnp.cos(angle) + first * jnp.sin(angle),
        ],
        axis=2,
    )
    return turned.reshape(block.shape[0], heads * HEAD_DIM).astype(jnp.bfloat16)


def project_joined(normed, weight, bias):
    grouped = lax.all_gather(normed, "gy", axis=0, tiled=True)
    summed = jnp.dot(
        grouped,
        lax.all_gather(weight, "gx", axis=0, tiled=True),
        preferred_element_type=jnp.float32,
    )
    width = weight.shape[1]
    bias_block = lax.dynamic_slice_in_dim(bias, lax.axis_index("gy") * width, width, 0)
    block_out = (summed + bias_block[None, :]).astype(jnp.bfloat16)
    return lax.all_to_all(block_out, "gy", split_axis=0, concat_axis=1, tiled=True)


def on_device(hidden_in, lengths, attn_norm, qkv_weight, qkv_bias):
    rows = hidden_in.shape[0]
    first = lax.axis_index("gy") * rows
    row_lengths = lengths[0]
    qdim = HEADS * HEAD_DIM
    kdim = KV_HEADS * HEAD_DIM
    group = HEADS // KV_HEADS
    normed = norm_rows(hidden_in, attn_norm)
    joined = project_joined(normed, qkv_weight, qkv_bias)
    ends = jnp.cumsum(row_lengths)
    tokens_here = first + jnp.arange(rows, dtype=jnp.int32)
    before = ends[None, :] <= tokens_here[:, None]
    seg_here = jnp.sum(before.astype(jnp.int32), axis=1)
    begin = jnp.sum(jnp.where(before, row_lengths[None, :], 0), axis=1)
    pos = tokens_here - begin
    queries = rotate(joined[:, :qdim], pos, HEADS).reshape(rows, KV_HEADS, group, HEAD_DIM)
    keys = rotate(joined[:, qdim : qdim + kdim], pos, KV_HEADS)
    kv_rows = jnp.concatenate([keys, joined[:, qdim + kdim :]], axis=1)
    scale = 1.0 / HEAD_DIM**0.5

    def attend(carry, piece, start):
        running, total, summed = carry
        key_count = piece.shape[0]
        key_index = start + jnp.arange(key_count, dtype=jnp.int32)
        key_seg = segment_of(key_index, ends)
        key_part = piece[:, :kdim].reshape(key_count, KV_HEADS, HEAD_DIM)
        value_part = piece[:, kdim:].reshape(key_count, KV_HEADS, HEAD_DIM)
        scores = (
            jnp.einsum("rgho,ngo->ghrn", queries, key_part, preferred_element_type=jnp.float32)
            * scale
        )
        allowed = (seg_here[:, None] == key_seg[None, :]) & (
            key_index[None, :] <= tokens_here[:, None]
        )
        newest = jnp.maximum(running, jnp.max(jnp.where(allowed, scores, -1e30), axis=3))
        shrink = jnp.exp(running - newest)
        weights = jnp.where(allowed, jnp.exp(scores - newest[..., None]), 0.0)
        total = total * shrink + jnp.sum(weights, axis=3)
        summed = summed * shrink[..., None] + jnp.einsum(
            "ghrn,ngo->ghro",
            weights.astype(jnp.bfloat16),
            value_part,
            preferred_element_type=jnp.float32,
        )
        return (newest, total, summed)

    def visit(carry, piece, start):
        return attend(carry, piece, start)

    start_state = (
        jnp.full((KV_HEADS, group, rows), -1e30, jnp.float32),
        jnp.zeros((KV_HEADS, group, rows), jnp.float32),
        jnp.zeros((KV_HEADS, group, rows, HEAD_DIM), jnp.float32),
    )
    piece = lax.all_gather(kv_rows, "gy", axis=0, tiled=True)
    length = piece.shape[0]
    span = math.gcd(length, key_span)
    stacked = piece.reshape(length // span, span, piece.shape[1])
    offsets = jnp.arange(length // span, dtype=jnp.int32) * span

    def advance(state, item):
        return (visit(state, item[0], item[1]), None)

    final_state, unused = lax.scan(advance, start_state, (stacked, offsets))
    running, total, summed = final_state
    attn = (
        jnp.transpose(summed / total[..., None], (2, 0, 1, 3))
        .reshape(rows, qdim)
        .astype(jnp.bfloat16)
    )
    return (attn, kv_rows)


def solution(mesh):
    placed = (P(("gx", "gy"), None), P("gx", None), P(), P("gx", "gy"), P())
    return jax.shard_map(
        on_device,
        mesh=mesh,
        in_specs=placed,
        out_specs=(P(("gx", "gy"), None), P(("gx", "gy"), None)),
        check_vma=False,
    )
```

profile of v0, /device:TPU:0, one launch (start us, length us, event | category | flops | bytes accessed | tf_op | source)
XLA Modules:
  0.0 595.3 jit_solution(592481126304964280)
XLA Ops:
  13.9 24.0 %all-gather.9.cloned.1.call-done = bf16[8,448,288]{1,2,0:T(8,128)(2,1)} async-done(((bf16[1,448,288]{1,2,0:T(8,128)(2,1)}), bf16[8,448,288]{1,2,0:T(8,128)(2,1)}) %all-gather.9.cloned.1.call-update) | async-done | bytes 2064400 | tf_op jit(solution)/shard_map/all_gather | solution.py:43
  44.5 172.0 %all-gather.5.cloned.1.call-done = bf16[4096,3584]{1,0:T(8,128)(2,1)} async-done(((bf16[256,3584]{1,0:T(8,128)(2,1)}), bf16[4096,3584]{1,0:T(8,128)(2,1)}) %all-gather.5.cloned.1.call-update) | async-done | bytes 29360144 | tf_op jit(solution)/shard_map/all_gather | solution.py:40
  216.6 14.7 %fusion.16 = bf16[4096,288]{0,1:T(8,128)(2,1)S(1)} fusion(bf16[4096,3584]{1,0:T(8,128)(2,1)} %all-gather.5.cloned.1.call-done, bf16[3584,288]{0,1:T(8,128)(2,1)} %reshape.172, f32[288]{0:T(512)S(1)} %dynamic_slice.11), kind=kOutput, calls=%fused_computation.25 | convolution fusion | flops 8458076160 | bytes 33784960 | tf_op jit(solution)/shard_map/dot_general | solution.py:41
  239.1 34.4 %all-to-all-done = bf16[16,256,288]{1,2,0:T(8,128)(2,1)S(1)} async-done(((bf16[16,256,288]{1,2,0:T(8,128)(2,1)}), bf16[16,256,288]{1,2,0:T(8,128)(2,1)S(1)}, u32[]{:S(2)}, u32[]{:S(2)}) %all-to-all-start) | async-done | bytes 2359328 | tf_op jit(solution)/shard_map/all_to_all | solution.py:49
  283.8 65.9 %all-gather.7.cloned.1.call-done = bf16[4096,1024]{0,1:T(8,128)(2,1)} async-done(((bf16[256,1024]{0,1:T(8,128)(2,1)}), bf16[4096,1024]{0,1:T(8,128)(2,1)}) %all-gather.7.cloned.1.call-update) | async-done | bytes 8388624 | tf_op jit(solution)/shard_map/all_gather | solution.py:106
  349.7 7.5 %copy.52 = bf16[128,8,8,512]{3,2,0,1:T(8,128)(2,1)} copy(bf16[128,8,8,512]{3,2,1,0:T(8,128)(2,1)} %bitcast.86) | data formatting | bytes 16777216 | tf_op jit(solution)/shard_map/reshape | solution.py:109
  357.2 222.0 %while.15 = (s32[]{:T(128)}, f32[4,7,256]{2,1,0:T(8,128)S(1)}, f32[4,7,256]{2,1,0:T(8,128)S(1)}, f32[4,7,256,128]{3,2,1,0:T(8,128)}, s32[256]{0:T(256)S(1)}, /*i...) while((s32[]{:T(128)}, f32[4,7,256]{2,1,0:T(8,128)S(1)}, ...), condition=%wide.region_8.9_spmd.clone, body=%wide.region_4.8_spmd.clone.sunk | while | flops 1922606336 | bytes 88814816 | solution.py:115
  366.6 8.3 %fusion.44 = f32[4,7,256]{2,1,0:T(8,128)S(1)} fusion(f32[4,512,256,7]{2,1,3,0:T(8,128)} %get-tuple-element.234, f32[4,7,256]{2,1,0:T(8,128)S(1)} %select_maximum_fusion.2, pred[256,512]{0,1:T(8,128)(4,1)S(1)} %compare_and_fusion.2), kind=kLoop, calls=%fused_computation.7.clone.1 | loop fusion | flops 14672896 | bytes 14868480 | tf_op jit(solution)/shard_map/while/body/eval_jaxpr/reduce_sum | solution.py:89
  375.0 8.0 %fusion.46 = f32[4,7,256,128]{3,2,1,0:T(8,128)S(1)} fusion(f32[4,7,256,128]{3,2,1,0:T(8,128)S(1)} %copy-done.1, bf16[512,4,128,1]{0,2,3,1:T(8,128)(2,1)S(1)} %bitcast.82, f32[4,512,256,7]{2,1,3,0:T(8,128)} %get-tuple-element.234, f32[4,7,256]{2,1,0:T(8,128)S(1)} %select_maximum_fusion.2, pred[256,512]{0,1:T(8,128)(4,1)S(1)} %compare_and_fusion.2, ...), kind=kOutput, calls=%fused_computation.11.clone.1 | convolution fusion | flops 956956672 | bytes 22732800 | tf_op jit(solution)/shard_map/while/body/eval_jaxpr/ghrn,ngo->ghro/dot_general | solution.py:90
  394.4 8.3 %fusion.44 = f32[4,7,256]{2,1,0:T(8,128)S(1)} fusion(f32[4,512,256,7]{2,1,3,0:T(8,128)} %get-tuple-element.234, f32[4,7,256]{2,1,0:T(8,128)S(1)} %select_maximum_fusion.2, pred[256,512]{0,1:T(8,128)(4,1)S(1)} %compare_and_fusion.2), kind=kLoop, calls=%fused_computation.7.clone.1 | loop fusion | flops 14672896 | bytes 14868480 | tf_op jit(solution)/shard_map/while/body/eval_jaxpr/reduce_sum | solution.py:89
  402.7 8.0 %fusion.46 = f32[4,7,256,128]{3,2,1,0:T(8,128)S(1)} fusion(f32[4,7,256,128]{3,2,1,0:T(8,128)S(1)} %copy-done.1, bf16[512,4,128,1]{0,2,3,1:T(8,128)(2,1)S(1)} %bitcast.82, f32[4,512,256,7]{2,1,3,0:T(8,128)} %get-tuple-element.234, f32[4,7,256]{2,1,0:T(8,128)S(1)} %select_maximum_fusion.2, pred[256,512]{0,1:T(8,128)(4,1)S(1)} %compare_and_fusion.2, ...), kind=kOutput, calls=%fused_computation.11.clone.1 | convolution fusion | flops 956956672 | bytes 22732800 | tf_op jit(solution)/shard_map/while/body/eval_jaxpr/ghrn,ngo->ghro/dot_general | solution.py:90
  422.1 8.3 %fusion.44 = f32[4,7,256]{2,1,0:T(8,128)S(1)} fusion(f32[4,512,256,7]{2,1,3,0:T(8,128)} %get-tuple-element.234, f32[4,7,256]{2,1,0:T(8,128)S(1)} %select_maximum_fusion.2, pred[256,512]{0,1:T(8,128)(4,1)S(1)} %compare_and_fusion.2), kind=kLoop, calls=%fused_computation.7.clone.1 | loop fusion | flops 14672896 | bytes 14868480 | tf_op jit(solution)/shard_map/while/body/eval_jaxpr/reduce_sum | solution.py:89
  430.5 8.0 %fusion.46 = f32[4,7,256,128]{3,2,1,0:T(8,128)S(1)} fusion(f32[4,7,256,128]{3,2,1,0:T(8,128)S(1)} %copy-done.1, bf16[512,4,128,1]{0,2,3,1:T(8,128)(2,1)S(1)} %bitcast.82, f32[4,512,256,7]{2,1,3,0:T(8,128)} %get-tuple-element.234, f32[4,7,256]{2,1,0:T(8,128)S(1)} %select_maximum_fusion.2, pred[256,512]{0,1:T(8,128)(4,1)S(1)} %compare_and_fusion.2, ...), kind=kOutput, calls=%fused_computation.11.clone.1 | convolution fusion | flops 956956672 | bytes 22732800 | tf_op jit(solution)/shard_map/while/body/eval_jaxpr/ghrn,ngo->ghro/dot_general | solution.py:90
  449.9 8.3 %fusion.44 = f32[4,7,256]{2,1,0:T(8,128)S(1)} fusion(f32[4,512,256,7]{2,1,3,0:T(8,128)} %get-tuple-element.234, f32[4,7,256]{2,1,0:T(8,128)S(1)} %select_maximum_fusion.2, pred[256,512]{0,1:T(8,128)(4,1)S(1)} %compare_and_fusion.2), kind=kLoop, calls=%fused_computation.7.clone.1 | loop fusion | flops 14672896 | bytes 14868480 | tf_op jit(solution)/shard_map/while/body/eval_jaxpr/reduce_sum | solution.py:89
  458.2 8.0 %fusion.46 = f32[4,7,256,128]{3,2,1,0:T(8,128)S(1)} fusion(f32[4,7,256,128]{3,2,1,0:T(8,128)S(1)} %copy-done.1, bf16[512,4,128,1]{0,2,3,1:T(8,128)(2,1)S(1)} %bitcast.82, f32[4,512,256,7]{2,1,3,0:T(8,128)} %get-tuple-element.234, f32[4,7,256]{2,1,0:T(8,128)S(1)} %select_maximum_fusion.2, pred[256,512]{0,1:T(8,128)(4,1)S(1)} %compare_and_fusion.2, ...), kind=kOutput, calls=%fused_computation.11.clone.1 | convolution fusion | flops 956956672 | bytes 22732800 | tf_op jit(solution)/shard_map/while/body/eval_jaxpr/ghrn,ngo->ghro/dot_general | solution.py:90
  477.6 8.3 %fusion.44 = f32[4,7,256]{2,1,0:T(8,128)S(1)} fusion(f32[4,512,256,7]{2,1,3,0:T(8,128)} %get-tuple-element.234, f32[4,7,256]{2,1,0:T(8,128)S(1)} %select_maximum_fusion.2, pred[256,512]{0,1:T(8,128)(4,1)S(1)} %compare_and_fusion.2), kind=kLoop, calls=%fused_computation.7.clone.1 | loop fusion | flops 14672896 | bytes 14868480 | tf_op jit(solution)/shard_map/while/body/eval_jaxpr/reduce_sum | solution.py:89
  486.0 8.0 %fusion.46 = f32[4,7,256,128]{3,2,1,0:T(8,128)S(1)} fusion(f32[4,7,256,128]{3,2,1,0:T(8,128)S(1)} %copy-done.1, bf16[512,4,128,1]{0,2,3,1:T(8,128)(2,1)S(1)} %bitcast.82, f32[4,512,256,7]{2,1,3,0:T(8,128)} %get-tuple-element.234, f32[4,7,256]{2,1,0:T(8,128)S(1)} %select_maximum_fusion.2, pred[256,512]{0,1:T(8,128)(4,1)S(1)} %compare_and_fusion.2, ...), kind=kOutput, calls=%fused_computation.11.clone.1 | convolution fusion | flops 956956672 | bytes 22732800 | tf_op jit(solution)/shard_map/while/body/eval_jaxpr/ghrn,ngo->ghro/dot_general | solution.py:90
  505.4 8.3 %fusion.44 = f32[4,7,256]{2,1,0:T(8,128)S(1)} fusion(f32[4,512,256,7]{2,1,3,0:T(8,128)} %get-tuple-element.234, f32[4,7,256]{2,1,0:T(8,128)S(1)} %select_maximum_fusion.2, pred[256,512]{0,1:T(8,128)(4,1)S(1)} %compare_and_fusion.2), kind=kLoop, calls=%fused_computation.7.clone.1 | loop fusion | flops 14672896 | bytes 14868480 | tf_op jit(solution)/shard_map/while/body/eval_jaxpr/reduce_sum | solution.py:89
  513.7 8.0 %fusion.46 = f32[4,7,256,128]{3,2,1,0:T(8,128)S(1)} fusion(f32[4,7,256,128]{3,2,1,0:T(8,128)S(1)} %copy-done.1, bf16[512,4,128,1]{0,2,3,1:T(8,128)(2,1)S(1)} %bitcast.82, f32[4,512,256,7]{2,1,3,0:T(8,128)} %get-tuple-element.234, f32[4,7,256]{2,1,0:T(8,128)S(1)} %select_maximum_fusion.2, pred[256,512]{0,1:T(8,128)(4,1)S(1)} %compare_and_fusion.2, ...), kind=kOutput, calls=%fused_computation.11.clone.1 | convolution fusion | flops 956956672 | bytes 22732800 | tf_op jit(solution)/shard_map/while/body/eval_jaxpr/ghrn,ngo->ghro/dot_general | solution.py:90
  526.6 6.5 %fusion.43 = (f32[4,7,256]{2,1,0:T(8,128)S(1)}, f32[4,512,256,7]{2,1,3,0:T(8,128)}) fusion(pred[256,512]{0,1:T(8,128)(4,1)S(1)} %compare_and_fusion.2, bf16[512,4,128,1]{0,2,3,1:T(8,128)(2,1)S(1)} %bitcast.80, bf16[256,4,7,128]{3,0,2,1:T(8,128)(2,1)S(1)} %get-tuple-element.270), kind=kOutput, calls=%fused_computation.3.clone.1 | convolution fusion | flops 950526976 | bytes 17199104 | tf_op jit(solution)/shard_map/while/body/eval_jaxpr/rgho,ngo->ghrn/dot_general | solution.py:80
  533.1 8.3 %fusion.44 = f32[4,7,256]{2,1,0:T(8,128)S(1)} fusion(f32[4,512,256,7]{2,1,3,0:T(8,128)} %get-tuple-element.234, f32[4,7,256]{2,1,0:T(8,128)S(1)} %select_maximum_fusion.2, pred[256,512]{0,1:T(8,128)(4,1)S(1)} %compare_and_fusion.2), kind=kLoop, calls=%fused_computation.7.clone.1 | loop fusion | flops 14672896 | bytes 14868480 | tf_op jit(solution)/shard_map/while/body/eval_jaxpr/reduce_sum | solution.py:89
  541.5 8.0 %fusion.46 = f32[4,7,256,128]{3,2,1,0:T(8,128)S(1)} fusion(f32[4,7,256,128]{3,2,1,0:T(8,128)S(1)} %copy-done.1, bf16[512,4,128,1]{0,2,3,1:T(8,128)(2,1)S(1)} %bitcast.82, f32[4,512,256,7]{2,1,3,0:T(8,128)} %get-tuple-element.234, f32[4,7,256]{2,1,0:T(8,128)S(1)} %select_maximum_fusion.2, pred[256,512]{0,1:T(8,128)(4,1)S(1)} %compare_and_fusion.2, ...), kind=kOutput, calls=%fused_computation.11.clone.1 | convolution fusion | flops 956956672 | bytes 22732800 | tf_op jit(solution)/shard_map/while/body/eval_jaxpr/ghrn,ngo->ghro/dot_general | solution.py:90
  560.9 8.3 %fusion.44 = f32[4,7,256]{2,1,0:T(8,128)S(1)} fusion(f32[4,512,256,7]{2,1,3,0:T(8,128)} %get-tuple-element.234, f32[4,7,256]{2,1,0:T(8,128)S(1)} %select_maximum_fusion.2, pred[256,512]{0,1:T(8,128)(4,1)S(1)} %compare_and_fusion.2), kind=kLoop, calls=%fused_computation.7.clone.1 | loop fusion | flops 14672896 | bytes 14868480 | tf_op jit(solution)/shard_map/while/body/eval_jaxpr/reduce_sum | solution.py:89
  569.2 8.0 %fusion.46 = f32[4,7,256,128]{3,2,1,0:T(8,128)S(1)} fusion(f32[4,7,256,128]{3,2,1,0:T(8,128)S(1)} %copy-done.1, bf16[512,4,128,1]{0,2,3,1:T(8,128)(2,1)S(1)} %bitcast.82, f32[4,512,256,7]{2,1,3,0:T(8,128)} %get-tuple-element.234, f32[4,7,256]{2,1,0:T(8,128)S(1)} %select_maximum_fusion.2, pred[256,512]{0,1:T(8,128)(4,1)S(1)} %compare_and_fusion.2, ...), kind=kOutput, calls=%fused_computation.11.clone.1 | convolution fusion | flops 956956672 | bytes 22732800 | tf_op jit(solution)/shard_map/while/body/eval_jaxpr/ghrn,ngo->ghro/dot_general | solution.py:90
  (161 shorter events, 125.2 us)
Async XLA Ops:
  7.2 30.8 %all-gather.9.cloned.1.call-start = ((), (), s32[]{:S(2)}) async-start(), calls=%async_computation.3 | async-start | bytes 2654208 | tf_op jit(solution)/shard_map/all_gather | solution.py:43
  7.9 208.7 %all-gather.5.cloned.1.call-start = ((), (), s32[]{:S(2)}) async-start(), calls=%async_computation.1 | async-start | bytes 31195136 | tf_op jit(solution)/shard_map/all_gather | solution.py:40
  231.3 7.2 %copy-start.3 = (s32[1,4]{1,0:T(1,128)S(1)}, s32[1,4]{1,0:T(1,128)}, u32[]{:S(2)}) copy-start(s32[1,4]{1,0:T(1,128)} %param.8) | copy-start | bytes 52
  233.0 40.5 %all-to-all-start = ((bf16[16,256,288]{1,2,0:T(8,128)(2,1)}), bf16[16,256,288]{1,2,0:T(8,128)(2,1)S(1)}, u32[]{:S(2)}, u32[]{:S(2)}) async-start(bf16[16,256,288]{1,2,0:T(8,128)(2,1)} %bitcast.85), calls=%async_computation | async-start | bytes 4718592 | tf_op jit(solution)/shard_map/all_to_all | solution.py:49
  238.2 111.5 %all-gather.7.cloned.1.call-start = ((), (), s32[]{:S(2)}) async-start(), calls=%async_computation.2 | async-start | bytes 8912896 | tf_op jit(solution)/shard_map/all_gather | solution.py:106
  274.5 1.4 copy-start
  366.6 8.4 %copy-start.1 = (f32[4,7,256,128]{3,2,1,0:T(8,128)S(1)}, f32[4,7,256,128]{3,2,1,0:T(8,128)}, u32[]{:S(2)}) copy-start(f32[4,7,256,128]{3,2,1,0:T(8,128)} %get-tuple-element.253) | copy-start | bytes 11010052 | tf_op jit(solution)/shard_map/while
  383.0 1.9 copy-start.2
  394.4 8.4 %copy-start.1 = (f32[4,7,256,128]{3,2,1,0:T(8,128)S(1)}, f32[4,7,256,128]{3,2,1,0:T(8,128)}, u32[]{:S(2)}) copy-start(f32[4,7,256,128]{3,2,1,0:T(8,128)} %get-tuple-element.253) | copy-start | bytes 11010052 | tf_op jit(solution)/shard_map/while
  410.8 1.9 copy-start.2
  422.1 8.4 %copy-start.1 = (f32[4,7,256,128]{3,2,1,0:T(8,128)S(1)}, f32[4,7,256,128]{3,2,1,0:T(8,128)}, u32[]{:S(2)}) copy-start(f32[4,7,256,128]{3,2,1,0:T(8,128)} %get-tuple-element.253) | copy-start | bytes 11010052 | tf_op jit(solution)/shard_map/while
  438.5 1.9 copy-start.2
  449.9 8.4 %copy-start.1 = (f32[4,7,256,128]{3,2,1,0:T(8,128)S(1)}, f32[4,7,256,128]{3,2,1,0:T(8,128)}, u32[]{:S(2)}) copy-start(f32[4,7,256,128]{3,2,1,0:T(8,128)} %get-tuple-element.253) | copy-start | bytes 11010052 | tf_op jit(solution)/shard_map/while
  466.3 1.9 copy-start.2
  477.6 8.4 %copy-start.1 = (f32[4,7,256,128]{3,2,1,0:T(8,128)S(1)}, f32[4,7,256,128]{3,2,1,0:T(8,128)}, u32[]{:S(2)}) copy-start(f32[4,7,256,128]{3,2,1,0:T(8,128)} %get-tuple-element.253) | copy-start | bytes 11010052 | tf_op jit(solution)/shard_map/while
  494.0 1.9 copy-start.2
  505.4 8.4 %copy-start.1 = (f32[4,7,256,128]{3,2,1,0:T(8,128)S(1)}, f32[4,7,256,128]{3,2,1,0:T(8,128)}, u32[]{:S(2)}) copy-start(f32[4,7,256,128]{3,2,1,0:T(8,128)} %get-tuple-element.253) | copy-start | bytes 11010052 | tf_op jit(solution)/shard_map/while
  521.8 1.9 copy-start.2
  533.1 8.4 %copy-start.1 = (f32[4,7,256,128]{3,2,1,0:T(8,128)S(1)}, f32[4,7,256,128]{3,2,1,0:T(8,128)}, u32[]{:S(2)}) copy-start(f32[4,7,256,128]{3,2,1,0:T(8,128)} %get-tuple-element.253) | copy-start | bytes 11010052 | tf_op jit(solution)/shard_map/while
  549.5 1.9 copy-start.2
  560.9 8.4 %copy-start.1 = (f32[4,7,256,128]{3,2,1,0:T(8,128)S(1)}, f32[4,7,256,128]{3,2,1,0:T(8,128)}, u32[]{:S(2)}) copy-start(f32[4,7,256,128]{3,2,1,0:T(8,128)} %get-tuple-element.253) | copy-start | bytes 11010052 | tf_op jit(solution)/shard_map/while
  577.3 1.9 copy-start.2
Sparse Core Ops, SparseCore 0:
  9.7 28.2 all-gather.8
  40.7 175.8 all-gather.4
  274.6 75.0 all-gather.6
where the time goes:
time: 597 us; the launch traced here: 595 us
  waiting for transfers between devices  297 us (50%)
  matrix products  131 us (22%)
  other arithmetic  87.5 us (15%)
  local copies, waits for them, and re-layouts  59.6 us (10%)
  between operations  13.9 us (2%)
    all_gather x1, waiting for transfers between devices, project_joined(): grouped = lax.all_gather(normed, 'gy', axis=0, tiled=True)  172 us
    reduce_sum x8, other arithmetic, attend(): total = total * shrink + jnp.sum(weights, axis=3)  66.5 us
    all_gather x1, waiting for transfers between devices, on_device(): piece = lax.all_gather(kv_rows, 'gy', axis=0, tiled=True)  65.9 us
    dot_general x8, matrix products, attend(): jnp.einsum('ghrn,ngo->ghro', weights.astype(jnp.bfloat16), value_part, pr...  64.3 us
    dot_general x8, matrix products, attend(): jnp.einsum('rgho,ngo->ghrn', queries, key_part, preferred_element_type=jn...  52.3 us
    all_to_all x1, waiting for transfers between devices, project_joined(): lax.all_to_all(block_out, 'gy', split_axis=0, concat_axis=1, tiled=True)  34.4 us
    all_gather x1, waiting for transfers between devices, project_joined(): lax.all_gather(weight, 'gx', axis=0, tiled=True)  24 us
    while x40, local copies, waits for them, and re-layouts  15 us
  transfers between devices with their start and end apart: 4, of which 4 were waited for; matrix products, arithmetic and copies ran while one was open for 4% of the time, Pallas kernels for 0%

commit v1 on v0

--- a/solution.py
+++ b/solution.py
@@ -8,6 +8,19 @@
 KV_HEADS = 4
 HEAD_DIM = 128
 key_span = 512
+
+
+def collect(array, axis, dim):
+    ways = lax.axis_size(axis)
+    up = [(d, (d + 1) % ways) for d in range(ways)]
+    down = [(d, (d - 1) % ways) for d in range(ways)]
+    earlier, later = ([array], [array])
+    for _ in range(ways // 2):
+        earlier.append(lax.ppermute(earlier[-1], axis, up))
+    for _ in range((ways - 1) // 2):
+        later.append(lax.ppermute(later[-1], axis, down))
+    line = jnp.concatenate([*earlier[::-1], *later[1:]], axis=dim)
+    return jnp.roll(line, (lax.axis_index(axis) - ways // 2) * array.shape[dim], axis=dim)
 
 
 def norm_rows(values, gain):
@@ -38,11 +51,7 @@
 
 def project_joined(normed, weight, bias):
     grouped = lax.all_gather(normed, "gy", axis=0, tiled=True)
-    summed = jnp.dot(
-        grouped,
-        lax.all_gather(weight, "gx", axis=0, tiled=True),
-        preferred_element_type=jnp.float32,
-    )
+    summed = jnp.dot(grouped, collect(weight, "gx", 0), preferred_element_type=jnp.float32)
     width = weight.shape[1]
     bias_block = lax.dynamic_slice_in_dim(bias, lax.axis_index("gy") * width, width, 0)
     block_out = (summed + bias_block[None, :]).astype(jnp.bfloat16)

time: 597 us -> 570 us (0.955)
  waiting for transfers between devices: 297 us -> 263 us
  starting transfers between devices: 5.55 us -> 15.1 us
    all_gather x1, waiting for transfers between devices: 172 us -> 143 us  [project_joined(): grouped = lax.all_gather(normed, 'gy', axis=0, tiled=True)]
    all_gather x1 -> x0, waiting for transfers between devices: 24 us -> none  [project_joined(): lax.all_gather(weight, 'gx', axis=0, tiled=True)]
    ppermute x0 -> x7, waiting for transfers between devices: none -> 19.7 us  [the longest x4 19.7 us: collect(): earlier.append(lax.ppermute(earlier[-1], axis, up))]
    ppermute x0 -> x7, starting transfers between devices: none -> 9.57 us  [the longest x3 9.54 us: collect(): later.append(lax.ppermute(later[-1], axis, down))]
  transfers between devices with their start and end apart: 4 -> 10, of which waited for: 4 -> 7; matrix products, arithmetic and copies ran while one was open for 4% -> 3% of each run, Pallas kernels for 0% -> 0%
where the time goes in v1:
time: 570 us; the launch traced here: 569 us
  waiting for transfers between devices  263 us (46%)
  matrix products  131 us (23%)
  other arithmetic  87.5 us (15%)
  local copies, waits for them, and re-layouts  58.1 us (10%)
  starting transfers between devices  15.1 us (3%)
  between operations  14.2 us (2%)
    all_gather x1, waiting for transfers between devices, project_joined(): grouped = lax.all_gather(normed, 'gy', axis=0, tiled=True)  143 us
    reduce_sum x8, other arithmetic, attend(): total = total * shrink + jnp.sum(weights, axis=3)  66.5 us
    all_gather x1, waiting for transfers between devices, on_device(): piece = lax.all_gather(kv_rows, 'gy', axis=0, tiled=True)  66 us
    dot_general x8, matrix products, attend(): jnp.einsum('ghrn,ngo->ghro', weights.astype(jnp.bfloat16), value_part, pr...  64.3 us
    dot_general x8, matrix products, attend(): jnp.einsum('rgho,ngo->ghrn', queries, key_part, preferred_element_type=jn...  51.8 us
    all_to_all x1, waiting for transfers between devices, project_joined(): lax.all_to_all(block_out, 'gy', split_axis=0, concat_axis=1, tiled=True)  34.4 us
    ppermute x4, waiting for transfers between devices, collect(): earlier.append(lax.ppermute(earlier[-1], axis, up))  19.7 us
    while x40, local copies, waits for them, and re-layouts  14.8 us
  transfers between devices with their start and end apart: 10, of which 7 were waited for; matrix products, arithmetic and copies ran while one was open for 3% of the time, Pallas kernels for 0%

profile of v1, /device:TPU:0, one launch (start us, length us, event | category | flops | bytes accessed | tf_op | source)
XLA Modules:
  0.0 569.1 jit_solution(3728094572263216327)
XLA Ops:
  36.0 6.6 %collective-permute-done.3 = bf16[448,288]{0,1:T(8,128)(2,1)S(1)} collective-permute-done((bf16[448,288]{0,1:T(8,128)(2,1)S(1)}, bf16[448,288]{0,1:T(8,128)(2,1)S(1)}, u32[]{:S(2)}, u32[]{:S(2)}) %collective-permute-start.3) | collective-permute-done | bytes 258080 | tf_op jit(solution)/shard_map/ppermute | solution.py:19
  47.7 142.8 %all-gather.3.cloned.1.call-done = bf16[4096,3584]{1,0:T(8,128)(2,1)} async-done(((bf16[256,3584]{1,0:T(8,128)(2,1)}), bf16[4096,3584]{1,0:T(8,128)(2,1)}) %all-gather.3.cloned.1.call-update) | async-done | bytes 29360144 | tf_op jit(solution)/shard_map/all_gather | solution.py:53
  190.5 14.8 %fusion.16 = bf16[4096,288]{0,1:T(8,128)(2,1)S(1)} fusion(bf16[4096,3584]{1,0:T(8,128)(2,1)} %all-gather.3.cloned.1.call-done, f32[288]{0:T(512)S(1)} %dynamic_slice.16, bf16[7168,288]{0,1:T(8,128)(2,1)} %concatenate.17, s32[]{:T(128)S(6)} %select_n.28), kind=kOutput, calls=%fused_computation.25 | convolution fusion | flops 8458076160 | bytes 33784964 | tf_op jit(solution)/shard_map/dot_general | solution.py:54
  213.1 34.4 %all-to-all-done = bf16[16,256,288]{1,2,0:T(8,128)(2,1)S(1)} async-done(((bf16[16,256,288]{1,2,0:T(8,128)(2,1)}), bf16[16,256,288]{1,2,0:T(8,128)(2,1)S(1)}, u32[]{:S(2)}, u32[]{:S(2)}) %all-to-all-start) | async-done | bytes 2359328 | tf_op jit(solution)/shard_map/all_to_all | solution.py:58
  257.8 66.0 %all-gather.5.cloned.1.call-done = bf16[4096,1024]{0,1:T(8,128)(2,1)} async-done(((bf16[256,1024]{0,1:T(8,128)(2,1)}), bf16[4096,1024]{0,1:T(8,128)(2,1)}) %all-gather.5.cloned.1.call-update) | async-done | bytes 8388624 | tf_op jit(solution)/shard_map/all_gather | solution.py:115
  323.8 7.5 %copy.40 = bf16[128,8,8,512]{3,2,0,1:T(8,128)(2,1)} copy(bf16[128,8,8,512]{3,2,1,0:T(8,128)(2,1)} %bitcast.82) | data formatting | bytes 16777216 | tf_op jit(solution)/shard_map/reshape | solution.py:118
  331.3 221.3 %while.15 = (s32[]{:T(128)}, f32[4,7,256]{2,1,0:T(8,128)S(1)}, f32[4,7,256]{2,1,0:T(8,128)S(1)}, f32[4,7,256,128]{3,2,1,0:T(8,128)}, s32[256]{0:T(256)S(1)}, /*i...) while((s32[]{:T(128)}, f32[4,7,256]{2,1,0:T(8,128)S(1)}, ...), condition=%wide.region_8.9_spmd.clone, body=%wide.region_4.8_spmd.clone.sunk | while | flops 1922606336 | bytes 88814816 | solution.py:124
  340.7 8.3 %fusion.45 = f32[4,7,256]{2,1,0:T(8,128)S(1)} fusion(f32[4,512,256,7]{2,1,3,0:T(8,128)} %get-tuple-element.222, f32[4,7,256]{2,1,0:T(8,128)S(1)} %select_maximum_fusion.2, pred[256,512]{0,1:T(8,128)(4,1)S(1)} %compare_and_fusion.2), kind=kLoop, calls=%fused_computation.7.clone.1 | loop fusion | flops 14672896 | bytes 14868480 | tf_op jit(solution)/shard_map/while/body/eval_jaxpr/reduce_sum | solution.py:98
  349.1 8.0 %fusion.47 = f32[4,7,256,128]{3,2,1,0:T(8,128)S(1)} fusion(f32[4,7,256,128]{3,2,1,0:T(8,128)S(1)} %copy-done.1, bf16[512,4,128,1]{0,2,3,1:T(8,128)(2,1)S(1)} %bitcast.78, f32[4,512,256,7]{2,1,3,0:T(8,128)} %get-tuple-element.222, f32[4,7,256]{2,1,0:T(8,128)S(1)} %select_maximum_fusion.2, pred[256,512]{0,1:T(8,128)(4,1)S(1)} %compare_and_fusion.2, ...), kind=kOutput, calls=%fused_computation.11.clone.1 | convolution fusion | flops 956956672 | bytes 22732800 | tf_op jit(solution)/shard_map/while/body/eval_jaxpr/ghrn,ngo->ghro/dot_general | solution.py:99
  361.9 6.5 %fusion.44 = (f32[4,7,256]{2,1,0:T(8,128)S(1)}, f32[4,512,256,7]{2,1,3,0:T(8,128)}) fusion(pred[256,512]{0,1:T(8,128)(4,1)S(1)} %compare_and_fusion.2, bf16[512,4,128,1]{0,2,3,1:T(8,128)(2,1)S(1)} %bitcast.76, bf16[256,4,7,128]{3,0,2,1:T(8,128)(2,1)S(1)} %get-tuple-element.258), kind=kOutput, calls=%fused_computation.3.clone.1 | convolution fusion | flops 950526976 | bytes 17199104 | tf_op jit(solution)/shard_map/while/body/eval_jaxpr/rgho,ngo->ghrn/dot_general | solution.py:89
  368.4 8.3 %fusion.45 = f32[4,7,256]{2,1,0:T(8,128)S(1)} fusion(f32[4,512,256,7]{2,1,3,0:T(8,128)} %get-tuple-element.222, f32[4,7,256]{2,1,0:T(8,128)S(1)} %select_maximum_fusion.2, pred[256,512]{0,1:T(8,128)(4,1)S(1)} %compare_and_fusion.2), kind=kLoop, calls=%fused_computation.7.clone.1 | loop fusion | flops 14672896 | bytes 14868480 | tf_op jit(solution)/shard_map/while/body/eval_jaxpr/reduce_sum | solution.py:98
  376.7 8.0 %fusion.47 = f32[4,7,256,128]{3,2,1,0:T(8,128)S(1)} fusion(f32[4,7,256,128]{3,2,1,0:T(8,128)S(1)} %copy-done.1, bf16[512,4,128,1]{0,2,3,1:T(8,128)(2,1)S(1)} %bitcast.78, f32[4,512,256,7]{2,1,3,0:T(8,128)} %get-tuple-element.222, f32[4,7,256]{2,1,0:T(8,128)S(1)} %select_maximum_fusion.2, pred[256,512]{0,1:T(8,128)(4,1)S(1)} %compare_and_fusion.2, ...), kind=kOutput, calls=%fused_computation.11.clone.1 | convolution fusion | flops 956956672 | bytes 22732800 | tf_op jit(solution)/shard_map/while/body/eval_jaxpr/ghrn,ngo->ghro/dot_general | solution.py:99
  396.0 8.3 %fusion.45 = f32[4,7,256]{2,1,0:T(8,128)S(1)} fusion(f32[4,512,256,7]{2,1,3,0:T(8,128)} %get-tuple-element.222, f32[4,7,256]{2,1,0:T(8,128)S(1)} %select_maximum_fusion.2, pred[256,512]{0,1:T(8,128)(4,1)S(1)} %compare_and_fusion.2), kind=kLoop, calls=%fused_computation.7.clone.1 | loop fusion | flops 14672896 | bytes 14868480 | tf_op jit(solution)/shard_map/while/body/eval_jaxpr/reduce_sum | solution.py:98
  404.4 8.0 %fusion.47 = f32[4,7,256,128]{3,2,1,0:T(8,128)S(1)} fusion(f32[4,7,256,128]{3,2,1,0:T(8,128)S(1)} %copy-done.1, bf16[512,4,128,1]{0,2,3,1:T(8,128)(2,1)S(1)} %bitcast.78, f32[4,512,256,7]{2,1,3,0:T(8,128)} %get-tuple-element.222, f32[4,7,256]{2,1,0:T(8,128)S(1)} %select_maximum_fusion.2, pred[256,512]{0,1:T(8,128)(4,1)S(1)} %compare_and_fusion.2, ...), kind=kOutput, calls=%fused_computation.11.clone.1 | convolution fusion | flops 956956672 | bytes 22732800 | tf_op jit(solution)/shard_map/while/body/eval_jaxpr/ghrn,ngo->ghro/dot_general | solution.py:99
  423.7 8.3 %fusion.45 = f32[4,7,256]{2,1,0:T(8,128)S(1)} fusion(f32[4,512,256,7]{2,1,3,0:T(8,128)} %get-tuple-element.222, f32[4,7,256]{2,1,0:T(8,128)S(1)} %select_maximum_fusion.2, pred[256,512]{0,1:T(8,128)(4,1)S(1)} %compare_and_fusion.2), kind=kLoop, calls=%fused_computation.7.clone.1 | loop fusion | flops 14672896 | bytes 14868480 | tf_op jit(solution)/shard_map/while/body/eval_jaxpr/reduce_sum | solution.py:98
  432.1 8.0 %fusion.47 = f32[4,7,256,128]{3,2,1,0:T(8,128)S(1)} fusion(f32[4,7,256,128]{3,2,1,0:T(8,128)S(1)} %copy-done.1, bf16[512,4,128,1]{0,2,3,1:T(8,128)(2,1)S(1)} %bitcast.78, f32[4,512,256,7]{2,1,3,0:T(8,128)} %get-tuple-element.222, f32[4,7,256]{2,1,0:T(8,128)S(1)} %select_maximum_fusion.2, pred[256,512]{0,1:T(8,128)(4,1)S(1)} %compare_and_fusion.2, ...), kind=kOutput, calls=%fused_computation.11.clone.1 | convolution fusion | flops 956956672 | bytes 22732800 | tf_op jit(solution)/shard_map/while/body/eval_jaxpr/ghrn,ngo->ghro/dot_general | solution.py:99
  451.4 8.3 %fusion.45 = f32[4,7,256]{2,1,0:T(8,128)S(1)} fusion(f32[4,512,256,7]{2,1,3,0:T(8,128)} %get-tuple-element.222, f32[4,7,256]{2,1,0:T(8,128)S(1)} %select_maximum_fusion.2, pred[256,512]{0,1:T(8,128)(4,1)S(1)} %compare_and_fusion.2), kind=kLoop, calls=%fused_computation.7.clone.1 | loop fusion | flops 14672896 | bytes 14868480 | tf_op jit(solution)/shard_map/while/body/eval_jaxpr/reduce_sum | solution.py:98
  459.7 8.0 %fusion.47 = f32[4,7,256,128]{3,2,1,0:T(8,128)S(1)} fusion(f32[4,7,256,128]{3,2,1,0:T(8,128)S(1)} %copy-done.1, bf16[512,4,128,1]{0,2,3,1:T(8,128)(2,1)S(1)} %bitcast.78, f32[4,512,256,7]{2,1,3,0:T(8,128)} %get-tuple-element.222, f32[4,7,256]{2,1,0:T(8,128)S(1)} %select_maximum_fusion.2, pred[256,512]{0,1:T(8,128)(4,1)S(1)} %compare_and_fusion.2, ...), kind=kOutput, calls=%fused_computation.11.clone.1 | convolution fusion | flops 956956672 | bytes 22732800 | tf_op jit(solution)/shard_map/while/body/eval_jaxpr/ghrn,ngo->ghro/dot_general | solution.py:99
  479.0 8.3 %fusion.45 = f32[4,7,256]{2,1,0:T(8,128)S(1)} fusion(f32[4,512,256,7]{2,1,3,0:T(8,128)} %get-tuple-element.222, f32[4,7,256]{2,1,0:T(8,128)S(1)} %select_maximum_fusion.2, pred[256,512]{0,1:T(8,128)(4,1)S(1)} %compare_and_fusion.2), kind=kLoop, calls=%fused_computation.7.clone.1 | loop fusion | flops 14672896 | bytes 14868480 | tf_op jit(solution)/shard_map/while/body/eval_jaxpr/reduce_sum | solution.py:98
  487.4 8.0 %fusion.47 = f32[4,7,256,128]{3,2,1,0:T(8,128)S(1)} fusion(f32[4,7,256,128]{3,2,1,0:T(8,128)S(1)} %copy-done.1, bf16[512,4,128,1]{0,2,3,1:T(8,128)(2,1)S(1)} %bitcast.78, f32[4,512,256,7]{2,1,3,0:T(8,128)} %get-tuple-element.222, f32[4,7,256]{2,1,0:T(8,128)S(1)} %select_maximum_fusion.2, pred[256,512]{0,1:T(8,128)(4,1)S(1)} %compare_and_fusion.2, ...), kind=kOutput, calls=%fused_computation.11.clone.1 | convolution fusion | flops 956956672 | bytes 22732800 | tf_op jit(solution)/shard_map/while/body/eval_jaxpr/ghrn,ngo->ghro/dot_general | solution.py:99
  506.7 8.3 %fusion.45 = f32[4,7,256]{2,1,0:T(8,128)S(1)} fusion(f32[4,512,256,7]{2,1,3,0:T(8,128)} %get-tuple-element.222, f32[4,7,256]{2,1,0:T(8,128)S(1)} %select_maximum_fusion.2, pred[256,512]{0,1:T(8,128)(4,1)S(1)} %compare_and_fusion.2), kind=kLoop, calls=%fused_computation.7.clone.1 | loop fusion | flops 14672896 | bytes 14868480 | tf_op jit(solution)/shard_map/while/body/eval_jaxpr/reduce_sum | solution.py:98
  515.0 8.0 %fusion.47 = f32[4,7,256,128]{3,2,1,0:T(8,128)S(1)} fusion(f32[4,7,256,128]{3,2,1,0:T(8,128)S(1)} %copy-done.1, bf16[512,4,128,1]{0,2,3,1:T(8,128)(2,1)S(1)} %bitcast.78, f32[4,512,256,7]{2,1,3,0:T(8,128)} %get-tuple-element.222, f32[4,7,256]{2,1,0:T(8,128)S(1)} %select_maximum_fusion.2, pred[256,512]{0,1:T(8,128)(4,1)S(1)} %compare_and_fusion.2, ...), kind=kOutput, calls=%fused_computation.11.clone.1 | convolution fusion | flops 956956672 | bytes 22732800 | tf_op jit(solution)/shard_map/while/body/eval_jaxpr/ghrn,ngo->ghro/dot_general | solution.py:99
  534.4 8.3 %fusion.45 = f32[4,7,256]{2,1,0:T(8,128)S(1)} fusion(f32[4,512,256,7]{2,1,3,0:T(8,128)} %get-tuple-element.222, f32[4,7,256]{2,1,0:T(8,128)S(1)} %select_maximum_fusion.2, pred[256,512]{0,1:T(8,128)(4,1)S(1)} %compare_and_fusion.2), kind=kLoop, calls=%fused_computation.7.clone.1 | loop fusion | flops 14672896 | bytes 14868480 | tf_op jit(solution)/shard_map/while/body/eval_jaxpr/reduce_sum | solution.py:98
  542.7 8.0 %fusion.47 = f32[4,7,256,128]{3,2,1,0:T(8,128)S(1)} fusion(f32[4,7,256,128]{3,2,1,0:T(8,128)S(1)} %copy-done.1, bf16[512,4,128,1]{0,2,3,1:T(8,128)(2,1)S(1)} %bitcast.78, f32[4,512,256,7]{2,1,3,0:T(8,128)} %get-tuple-element.222, f32[4,7,256]{2,1,0:T(8,128)S(1)} %select_maximum_fusion.2, pred[256,512]{0,1:T(8,128)(4,1)S(1)} %compare_and_fusion.2, ...), kind=kOutput, calls=%fused_computation.11.clone.1 | convolution fusion | flops 956956672 | bytes 22732800 | tf_op jit(solution)/shard_map/while/body/eval_jaxpr/ghrn,ngo->ghro/dot_general | solution.py:99
  (173 shorter events, 145.2 us)
Async XLA Ops:
  7.2 5.3 copy-start.3
  7.2 183.3 %all-gather.3.cloned.1.call-start = ((), (), s32[]{:S(2)}) async-start(), calls=%async_computation.1 | async-start | bytes 31195136 | tf_op jit(solution)/shard_map/all_gather | solution.py:53
  12.5 8.0 %collective-permute-start = (bf16[448,288]{0,1:T(8,128)(2,1)S(1)}, bf16[448,288]{0,1:T(8,128)(2,1)S(1)}, u32[]{:S(2)}, u32[]{:S(2)}) collective-permute-start(bf16[448,288]{0,1:T(8,128)(2,1)S(1)} %copy-done.3), channel_id=1, source_target_pairs={{0,16},{16,32},{32,48},{48,64},{64,80},{80,96},{96,112},{112,0},{1... | collective-permute-start | bytes 774152 | tf_op jit(solution)/shard_map/ppermute | solution.py:19
  12.5 8.0 %collective-permute-start.4 = (bf16[448,288]{0,1:T(8,128)(2,1)S(1)}, bf16[448,288]{0,1:T(8,128)(2,1)S(1)}, u32[]{:S(2)}, u32[]{:S(2)}) collective-permute-start(bf16[448,288]{0,1:T(8,128)(2,1)S(1)} %copy-done.3), channel_id=1, source_target_pairs={{0,112},{16,0},{32,16},{48,32},{64,48},{80,64},{96,80},{112,96},{1... | collective-permute-start | bytes 774152 | tf_op jit(solution)/shard_map/ppermute | solution.py:21
  20.5 7.4 %collective-permute-start.1 = (bf16[448,288]{0,1:T(8,128)(2,1)S(1)}, bf16[448,288]{0,1:T(8,128)(2,1)S(1)}, u32[]{:S(2)}, u32[]{:S(2)}) collective-permute-start(bf16[448,288]{0,1:T(8,128)(2,1)S(1)} %collective-permute-done), channel_id=1, source_target_pairs={{0,16},{16,32},{32,48},{48,64},{64,80},{80,96},{96,112},{112,0},{1... | collective-permute-start | bytes 774152 | tf_op jit(solution)/shard_map/ppermute | solution.py:19
  20.5 7.4 %collective-permute-start.5 = (bf16[448,288]{0,1:T(8,128)(2,1)S(1)}, bf16[448,288]{0,1:T(8,128)(2,1)S(1)}, u32[]{:S(2)}, u32[]{:S(2)}) collective-permute-start(bf16[448,288]{0,1:T(8,128)(2,1)S(1)} %collective-permute-done.4), channel_id=1, source_target_pairs={{0,112},{16,0},{32,16},{48,32},{64,48},{80,64},{96,80},{112,96},{1... | collective-permute-start | bytes 774152 | tf_op jit(solution)/shard_map/ppermute | solution.py:21
  27.9 7.4 %collective-permute-start.2 = (bf16[448,288]{0,1:T(8,128)(2,1)S(1)}, bf16[448,288]{0,1:T(8,128)(2,1)S(1)}, u32[]{:S(2)}, u32[]{:S(2)}) collective-permute-start(bf16[448,288]{0,1:T(8,128)(2,1)S(1)} %collective-permute-done.1), channel_id=1, source_target_pairs={{0,16},{16,32},{32,48},{48,64},{64,80},{80,96},{96,112},{112,0},{1... | collective-permute-start | bytes 774152 | tf_op jit(solution)/shard_map/ppermute | solution.py:19
  27.9 8.1 %collective-permute-start.6 = (bf16[448,288]{0,1:T(8,128)(2,1)S(1)}, bf16[448,288]{0,1:T(8,128)(2,1)S(1)}, u32[]{:S(2)}, u32[]{:S(2)}) collective-permute-start(bf16[448,288]{0,1:T(8,128)(2,1)S(1)} %collective-permute-done.5), channel_id=1, source_target_pairs={{0,112},{16,0},{32,16},{48,32},{64,48},{80,64},{96,80},{112,96},{1... | collective-permute-start | bytes 774152 | tf_op jit(solution)/shard_map/ppermute | solution.py:21
  35.2 7.4 %collective-permute-start.3 = (bf16[448,288]{0,1:T(8,128)(2,1)S(1)}, bf16[448,288]{0,1:T(8,128)(2,1)S(1)}, u32[]{:S(2)}, u32[]{:S(2)}) collective-permute-start(bf16[448,288]{0,1:T(8,128)(2,1)S(1)} %collective-permute-done.2), channel_id=1, source_target_pairs={{0,16},{16,32},{32,48},{48,64},{64,80},{80,96},{96,112},{112,0},{1... | collective-permute-start | bytes 774152 | tf_op jit(solution)/shard_map/ppermute | solution.py:19
  205.3 7.2 %copy-start.4 = (s32[1,4]{1,0:T(1,128)S(1)}, s32[1,4]{1,0:T(1,128)}, u32[]{:S(2)}) copy-start(s32[1,4]{1,0:T(1,128)} %param.8) | copy-start | bytes 52
  207.0 40.5 %all-to-all-start = ((bf16[16,256,288]{1,2,0:T(8,128)(2,1)}), bf16[16,256,288]{1,2,0:T(8,128)(2,1)S(1)}, u32[]{:S(2)}, u32[]{:S(2)}) async-start(bf16[16,256,288]{1,2,0:T(8,128)(2,1)} %bitcast.81), calls=%async_computation | async-start | bytes 4718592 | tf_op jit(solution)/shard_map/all_to_all | solution.py:58
  212.2 111.6 %all-gather.5.cloned.1.call-start = ((), (), s32[]{:S(2)}) async-start(), calls=%async_computation.2 | async-start | bytes 8912896 | tf_op jit(solution)/shard_map/all_gather | solution.py:115
  340.7 8.4 %copy-start.1 = (f32[4,7,256,128]{3,2,1,0:T(8,128)S(1)}, f32[4,7,256,128]{3,2,1,0:T(8,128)}, u32[]{:S(2)}) copy-start(f32[4,7,256,128]{3,2,1,0:T(8,128)} %get-tuple-element.241) | copy-start | bytes 11010052 | tf_op jit(solution)/shard_map/while
  357.1 1.9 copy-start.2
  368.4 8.4 %copy-start.1 = (f32[4,7,256,128]{3,2,1,0:T(8,128)S(1)}, f32[4,7,256,128]{3,2,1,0:T(8,128)}, u32[]{:S(2)}) copy-start(f32[4,7,256,128]{3,2,1,0:T(8,128)} %get-tuple-element.241) | copy-start | bytes 11010052 | tf_op jit(solution)/shard_map/while
  384.8 1.9 copy-start.2
  396.0 8.4 %copy-start.1 = (f32[4,7,256,128]{3,2,1,0:T(8,128)S(1)}, f32[4,7,256,128]{3,2,1,0:T(8,128)}, u32[]{:S(2)}) copy-start(f32[4,7,256,128]{3,2,1,0:T(8,128)} %get-tuple-element.241) | copy-start | bytes 11010052 | tf_op jit(solution)/shard_map/while
  412.4 1.9 copy-start.2
  423.7 8.4 %copy-start.1 = (f32[4,7,256,128]{3,2,1,0:T(8,128)S(1)}, f32[4,7,256,128]{3,2,1,0:T(8,128)}, u32[]{:S(2)}) copy-start(f32[4,7,256,128]{3,2,1,0:T(8,128)} %get-tuple-element.241) | copy-start | bytes 11010052 | tf_op jit(solution)/shard_map/while
  451.4 8.4 %copy-start.1 = (f32[4,7,256,128]{3,2,1,0:T(8,128)S(1)}, f32[4,7,256,128]{3,2,1,0:T(8,128)}, u32[]{:S(2)}) copy-start(f32[4,7,256,128]{3,2,1,0:T(8,128)} %get-tuple-element.241) | copy-start | bytes 11010052 | tf_op jit(solution)/shard_map/while
  479.0 8.4 %copy-start.1 = (f32[4,7,256,128]{3,2,1,0:T(8,128)S(1)}, f32[4,7,256,128]{3,2,1,0:T(8,128)}, u32[]{:S(2)}) copy-start(f32[4,7,256,128]{3,2,1,0:T(8,128)} %get-tuple-element.241) | copy-start | bytes 11010052 | tf_op jit(solution)/shard_map/while
  495.4 1.9 copy-start.2
  506.7 8.4 %copy-start.1 = (f32[4,7,256,128]{3,2,1,0:T(8,128)S(1)}, f32[4,7,256,128]{3,2,1,0:T(8,128)}, u32[]{:S(2)}) copy-start(f32[4,7,256,128]{3,2,1,0:T(8,128)} %get-tuple-element.241) | copy-start | bytes 11010052 | tf_op jit(solution)/shard_map/while
  534.4 8.4 %copy-start.1 = (f32[4,7,256,128]{3,2,1,0:T(8,128)S(1)}, f32[4,7,256,128]{3,2,1,0:T(8,128)}, u32[]{:S(2)}) copy-start(f32[4,7,256,128]{3,2,1,0:T(8,128)} %get-tuple-element.241) | copy-start | bytes 11010052 | tf_op jit(solution)/shard_map/while
  (5 other events, 8.8 us)
Sparse Core Ops, SparseCore 0:
  12.6 177.8 all-gather.2
  248.7 75.1 all-gather.4
